TPU v7x, 256 devices: a whole 4x4x8 slice. The times are simulated.
256 devices in a mesh: expert: 128 (over x, z, y), hid: 2 (over core).
Axes of the slice: x: 4, y: 4, z: 8, core: 2. Of those that a mesh axis runs over, the one named last changes fastest.
Arguments:
- tokens: bfloat16 [16384, 3584], P('expert'), may hold values from -6 to 6
- out_grad: bfloat16 [16384, 3584], P('expert'), may hold values from -4 to 4
- route_ids: int32 [16384, 4], P('expert'), may hold values from 0 to 127, all different within a row; in each aligned block of 128 rows (0 to 127, 128 to 255, ...) at most 6 rows name the same one
- route_gates: float32 [16384, 4], P('expert'), may hold values from 0.1 to 1
- w_gate: bfloat16 [128, 3584, 1024], P('expert', None, 'hid'), may hold values from -0.09375 to 0.09375
- w_up: bfloat16 [128, 3584, 1024], P('expert', None, 'hid'), may hold values from -0.09375 to 0.09375
- w_down: bfloat16 [128, 1024, 3584], P('expert', 'hid'), may hold values from -0.1875 to 0.1875
Outputs:
- token_grad: bfloat16 [16384, 3584], P('expert', 'hid')
- gate_grad: bfloat16 [16384, 4], P('expert')
Inputs may be any that keep to these rules, and one draw needn't show every extreme that they name: `route_ids`: each token names 4 different experts. Among the 128 tokens of one index of expert (aligned blocks of rows), no expert is named more than 6 times, a bound that some block reaches.
All inputs are finite; a program needn't handle non-finite values.
Results may differ from a plain program's by a relative error of at most 0.008.
Values may be sent and summed in bfloat16 or wider, within the bound.
No kernel may reach another device: no remote copies, remote signals or barrier semaphores. Data moves between devices by JAX's collectives and lax.ppermute only.
A program may use at most 128 MiB of HBM per device.

v0:
```python
import jax
import jax.numpy as jnp
from jax import lax
from jax.sharding import PartitionSpec as P


def body(tokens, out_grad, route_ids, route_gates, w_gate, w_up, w_down):
    expert_count = lax.axis_size("expert")
    pair_count = lax.axis_size("hid")
    hid_idx = lax.axis_index("hid")
    tok_rows, model_width = tokens.shape
    top_count = route_ids.shape[1]
    capacity = 3 * tok_rows * top_count // (2 * expert_count)
    slot_count = expert_count * capacity
    half_width = model_width // pair_count
    pair_total = tok_rows * top_count
    flat_ids = route_ids.reshape(-1)
    one_hot = (flat_ids[:, None] == jnp.arange(expert_count, dtype=jnp.int32)[None, :]).astype(
        jnp.int32
    )
    earlier = jnp.cumsum(one_hot, axis=0) - one_hot
    slot_index = jnp.sum(earlier * one_hot, axis=1)
    dest_slot = flat_ids * capacity + slot_index
    slot_pair = (
        jnp.zeros((slot_count,), jnp.int32)
        .at[dest_slot]
        .set(jnp.arange(pair_total, dtype=jnp.int32))
    )
    slot_token = slot_pair // top_count
    x_half = lax.dynamic_slice_in_dim(tokens, hid_idx * half_width, half_width, axis=1)
    d_half = lax.dynamic_slice_in_dim(out_grad, hid_idx * half_width, half_width, axis=1)
    send = jnp.stack([x_half[slot_token], d_half[slot_token]], axis=1).reshape(
        expert_count, capacity, 2, half_width
    )
    recv = lax.all_to_all(send, "expert", split_axis=0, concat_axis=0, tiled=True)
    full = lax.all_gather(recv, "hid", axis=3, tiled=True)
    rows_x = full[:, :, 0, :].reshape(slot_count, model_width)
    rows_d = full[:, :, 1, :].reshape(slot_count, model_width)
    gate_mat = w_gate[0]
    up_mat = w_up[0]
    down_mat = w_down[0]
    contract_last = (((1,), (1,)), ((), ()))
    gate_pre = jnp.dot(rows_x, gate_mat, preferred_element_type=jnp.float32)
    up_pre = jnp.dot(rows_x, up_mat, preferred_element_type=jnp.float32)
    grad_hidden = lax.dot_general(
        rows_d, down_mat, contract_last, preferred_element_type=jnp.float32
    )
    sigma_gate = jax.nn.sigmoid(gate_pre)
    act_gate = gate_pre * sigma_gate
    score_part = jnp.sum(act_gate * up_pre * grad_hidden, axis=1)
    grad_gate_pre = (
        grad_hidden * up_pre * sigma_gate * (1.0 + gate_pre * (1.0 - sigma_gate))
    ).astype(jnp.bfloat16)
    grad_up_pre = (grad_hidden * act_gate).astype(jnp.bfloat16)
    grad_part = lax.dot_general(
        grad_gate_pre, gate_mat, contract_last, preferred_element_type=jnp.float32
    ) + lax.dot_general(grad_up_pre, up_mat, contract_last, preferred_element_type=jnp.float32)
    grad_share = lax.psum_scatter(grad_part, "hid", scatter_dimension=1, tiled=True).astype(
        jnp.bfloat16
    )
    score_full = lax.psum(score_part, "hid").astype(jnp.bfloat16)
    back_grad, back_score = (
        lax.all_to_all(
            grad_share.reshape(expert_count, capacity, half_width),
            "expert",
            split_axis=0,
            concat_axis=0,
            tiled=True,
        ),
        lax.all_to_all(
            score_full.reshape(expert_count, capacity),
            "expert",
            split_axis=0,
            concat_axis=0,
            tiled=True,
        ),
    )
    picked = back_grad.reshape(slot_count, half_width)[dest_slot]
    picked = picked.reshape(tok_rows, top_count, half_width).astype(jnp.float32)
    token_grad = jnp.einsum("tkd,tk->td", picked, route_gates).astype(jnp.bfloat16)
    gate_grad = back_score.reshape(slot_count)[dest_slot].reshape(tok_rows, top_count)
    return (token_grad, gate_grad)


def solution(mesh):
    return jax.shard_map(
        body,
        mesh=mesh,
        in_specs=(
            P("expert", None),
            P("expert", None),
            P("expert", None),
            P("expert", None),
            P("expert", None, "hid"),
            P("expert", None, "hid"),
            P("expert", "hid", None),
        ),
        out_specs=(P("expert", "hid"), P("expert", None)),
        check_vma=False,
    )
```

profile of v0, /device:TPU:32, one launch (start us, length us, event | category | flops | bytes accessed | tf_op | source)
XLA Modules:
  0.0 480.9 jit_solution(7994707063346658145)
XLA Ops:
  13.5 4.1 gather_fusion
  17.6 5.4 %stack.9 = bf16[128,6,1,1792]{3,1,0,2:T(8,128)(2,1)} reshape(bf16[768,1792]{1,0:T(8,128)(2,1)} %gather_fusion) | data formatting | bytes 5505024 | tf_op jit(solution)/shard_map/stack | solution.py:32
  23.0 3.2 gather_fusion.1
  28.9 5.1 %pad_maximum_fusion = bf16[128,6,2,1792]{3,1,0,2:T(8,128)(2,1)S(1)} fusion(bf16[128,6,1,1792]{3,1,0,2:T(8,128)(2,1)} %stack.10, bf16[128,6,1,1792]{3,1,0,2:T(8,128)(2,1)} %stack.9), kind=kLoop, calls=%fused_computation.7 | loop fusion | flops 2752512 | bytes 11010048 | tf_op jit(solution)/shard_map/stack | solution.py:32
  34.0 25.1 %copy.20 = bf16[128,6,2,1792]{3,2,1,0:T(2,128)(2,1)S(1)} copy(bf16[128,6,2,1792]{3,1,0,2:T(8,128)(2,1)S(1)} %pad_maximum_fusion) | data formatting | bytes 11010048 | tf_op jit(solution)/shard_map/stack | solution.py:32
  59.2 140.6 %all_to_all.20 = bf16[128,6,2,1792]{3,2,1,0:T(2,128)(2,1)} all-to-all(bf16[128,6,2,1792]{3,2,1,0:T(2,128)(2,1)S(1)} %copy.20), channel_id=1, replica_groups=mesh['expert'=128,'hid'=2] {'expert'}, dimensions={0} | all-to-all | bytes 11010048 | tf_op jit(solution)/shard_map/all_to_all | solution.py:35
  199.9 23.1 %all-gather.2.cloned.1.call-done = bf16[128,6,2,3584]{3,2,1,0:T(2,128)(2,1)} async-done(((bf16[128,6,2,1792]{3,2,1,0:T(2,128)(2,1)}), bf16[128,6,2,3584]{3,2,1,0:T(2,128)(2,1)}) %all-gather.2.cloned.1.call-update) | async-done | bytes 11010064 | tf_op jit(solution)/shard_map/all_gather | solution.py:36
  223.0 59.4 %slice_reduce_fusion.1 = (bf16[128,6,3584]{2,1,0:T(8,128)(2,1)}, bf16[128,6,3584]{2,1,0:T(8,128)(2,1)}) fusion(bf16[128,6,2,3584]{3,2,1,0:T(2,128)(2,1)} %all-gather.2.cloned.1.call-done), kind=kLoop, calls=%fused_computation.6 | loop fusion | bytes 22020096 | tf_op jit(solution)/shard_map/slice | solution.py:38
  282.4 9.7 %reshape_squeeze.7 = bf16[768,3584]{1,0:T(8,128)(2,1)} reshape(bf16[128,6,3584]{2,1,0:T(8,128)(2,1)} %get-tuple-element.7) | data formatting | bytes 11010048 | tf_op jit(solution)/shard_map/reshape;squeeze | solution.py:37
  292.1 6.9 %fusion.2 = f32[768,512]{0,1:T(8,128)S(1)} fusion(bf16[768,3584]{1,0:T(8,128)(2,1)} %reshape_squeeze.7, bf16[1,3584,512]{2,1,0:T(8,128)(2,1)} %param.11), kind=kOutput, calls=%fused_computation.11 | convolution fusion | flops 2818572288 | bytes 10747904 | tf_op jit(solution)/shard_map/dot_general | solution.py:43
  299.0 3.1 fusion.5
  302.0 9.8 %reshape_squeeze.6 = bf16[768,3584]{1,0:T(8,128)(2,1)} reshape(bf16[128,6,3584]{2,1,0:T(8,128)(2,1)} %get-tuple-element.6) | data formatting | bytes 11010048 | tf_op jit(solution)/shard_map/reshape;squeeze | solution.py:38
  311.9 7.0 %multiply_reduce_fusion = (f32[768]{0:T(1024)S(1)}, f32[768,512]{0,1:T(8,128)S(1)}) fusion(f32[768,512]{0,1:T(8,128)S(1)} %fusion.5, f32[768,512]{0,1:T(8,128)S(1)} %fusion.2, bf16[768,3584]{1,0:T(8,128)(2,1)} %reshape_squeeze.6, bf16[1,512,3584]{2,1,0:T(8,128)(2,1)} %param.13), kind=kOutput, calls=%fused_computation.18 | convolution fusion | flops 2821324032 | bytes 13896704 | tf_op jit(solution)/shard_map/dot_general | solution.py:45
  318.9 3.6 fusion
  322.5 7.9 %convolution_add_fusion = f32[768,3584]{1,0:T(8,128)} fusion(f32[768,3584]{1,0:T(8,128)S(1)} %fusion, bf16[1,3584,512]{2,1,0:T(8,128)(2,1)} %param.12, f32[768,512]{0,1:T(8,128)S(1)} %get-tuple-element.9, f32[768,512]{0,1:T(8,128)S(1)} %fusion.2), kind=kOutput, calls=%fused_computation.8 | convolution fusion | flops 2823684096 | bytes 28835840 | tf_op jit(solution)/shard_map/dot_general | solution.py:57
  333.7 13.7 %all-to-all-start.2 = ((bf16[128,1,6]{2,1,0:T(2,128)(2,1)}), bf16[128,1,6]{2,1,0:T(2,128)(2,1)S(1)}, u32[]{:S(2)}, u32[]{:S(2)}) async-start(bf16[128,1,6]{2,1,0:T(2,128)(2,1)} %all_to_all.16), calls=%async_computation.3 | async-start | bytes 131072 | tf_op jit(solution)/shard_map/all_to_all | solution.py:70
  347.4 8.2 %reduce-scatter.2.cloned.1.call-done = f32[768,1792]{1,0:T(8,128)} async-done(((f32[768,3584]{1,0:T(8,128)}), f32[768,1792]{1,0:T(8,128)}) %reduce-scatter.2.cloned.1.call-update) | async-done | bytes 5505040 | tf_op jit(solution)/shard_map/reduce_scatter | solution.py:58
  355.6 2.8 convert_element_type.27
  361.1 14.6 %all-to-all-start.1 = ((bf16[128,6,1792]{2,1,0:T(8,128)(2,1)}), bf16[128,6,1792]{2,1,0:T(8,128)(2,1)}, u32[]{:S(2)}, u32[]{:S(2)}) async-start(bf16[128,6,1792]{2,1,0:T(8,128)(2,1)} %reshape.76), calls=%async_computation.2 | async-start | bytes 7340032 | tf_op jit(solution)/shard_map/all_to_all | solution.py:63
  376.3 3.5 gather_fusion.3
  380.6 81.1 %all-to-all-done.1 = bf16[128,6,1792]{2,1,0:T(8,128)(2,1)} async-done(((bf16[128,6,1792]{2,1,0:T(8,128)(2,1)}), bf16[128,6,1792]{2,1,0:T(8,128)(2,1)}, u32[]{:S(2)}, u32[]{:S(2)}) %all-to-all-start.1) | async-done | bytes 2752544 | tf_op jit(solution)/shard_map/all_to_all | solution.py:63
  461.7 4.0 reshape.77
  465.6 3.2 gather_fusion.2
  468.8 3.1 reshape.78
  (46 shorter events, 18.2 us)
Async XLA Ops:
  7.2 215.9 %all-gather.2.cloned.1.call-start = ((), (), s32[]{:S(2)}) async-start(), calls=%async_computation.4 | async-start | bytes 16515072 | tf_op jit(solution)/shard_map/all_gather | solution.py:36
  199.8 155.8 %reduce-scatter.2.cloned.1.call-start = ((), (), s32[]{:S(2)}) async-start(), calls=%async_computation.5 | async-start | bytes 16515072 | tf_op jit(solution)/shard_map/reduce_scatter | solution.py:58
  292.1 6.9 %copy-start = (bf16[768,3584]{1,0:T(8,128)(2,1)S(1)}, bf16[768,3584]{1,0:T(8,128)(2,1)}, u32[]{:S(2)}) copy-start(bf16[768,3584]{1,0:T(8,128)(2,1)} %reshape_squeeze.7) | copy-start | bytes 16515076
  292.1 6.9 %copy-start.2 = (bf16[1,3584,512]{2,1,0:T(8,128)(2,1)S(1)}, bf16[1,3584,512]{2,1,0:T(8,128)(2,1)}, u32[]{:S(2)}) copy-start(bf16[1,3584,512]{2,1,0:T(8,128)(2,1)} %param.12) | copy-start | bytes 11010052
  311.9 7.0 %copy-start.1 = (bf16[1,3584,512]{2,1,0:T(8,128)(2,1)S(1)}, bf16[1,3584,512]{2,1,0:T(8,128)(2,1)}, u32[]{:S(2)}) copy-start(bf16[1,3584,512]{2,1,0:T(8,128)(2,1)} %param.11) | copy-start | bytes 11010052
  333.7 27.4 %all-to-all-start.2 = ((bf16[128,1,6]{2,1,0:T(2,128)(2,1)}), bf16[128,1,6]{2,1,0:T(2,128)(2,1)S(1)}, u32[]{:S(2)}, u32[]{:S(2)}) async-start(bf16[128,1,6]{2,1,0:T(2,128)(2,1)} %all_to_all.16), calls=%async_computation.3 | async-start | bytes 131072 | tf_op jit(solution)/shard_map/all_to_all | solution.py:70
  361.1 14.6 %copy-start.3 = (f32[128,4]{0,1:T(4,128)S(1)}, f32[128,4]{0,1:T(4,128)}, u32[]{:S(2)}) copy-start(f32[128,4]{0,1:T(4,128)} %param.10) | copy-start | bytes 6148
  361.1 100.5 %all-to-all-start.1 = ((bf16[128,6,1792]{2,1,0:T(8,128)(2,1)}), bf16[128,6,1792]{2,1,0:T(8,128)(2,1)}, u32[]{:S(2)}, u32[]{:S(2)}) async-start(bf16[128,6,1792]{2,1,0:T(8,128)(2,1)} %reshape.76), calls=%async_computation.2 | async-start | bytes 7340032 | tf_op jit(solution)/shard_map/all_to_all | solution.py:63
Sparse Core Ops, SparseCore 0:
  200.0 23.0 all-gather.1
  330.6 24.9 reduce-scatter.1
where the time goes:
time: 490 us; the launch traced here: 481 us
  local copies, waits for them, and re-layouts  144 us (29%)
  blocking collectives  143 us (29%)
  waiting for transfers between devices  112 us (23%)
  matrix products  29.5 us (6%)
  starting transfers between devices  28.4 us (6%)
  between operations  14.5 us (3%)
  other arithmetic  9.33 us (2%)
    all_to_all x1, blocking collectives, body(): lax.all_to_all(send, 'expert', split_axis=0, concat_axis=0, tiled=True)  141 us
    all_to_all x1, waiting for transfers between devices, body(): lax.all_to_all(grad_share.reshape(expert_count, capacity, half_width), 'e...  81.1 us
    slice x1, local copies, waits for them, and re-layouts, body(): rows_d = full[:, :, 1, :].reshape(slot_count, model_width)  59.4 us
    another operation x3, local copies, waits for them, and re-layouts, body(): jnp.stack([x_half[slot_token], d_half[slot_token]], axis=1)  33.3 us
    all_gather x1, waiting for transfers between devices, body(): full = lax.all_gather(recv, 'hid', axis=3, tiled=True)  23.1 us
    all_to_all x1, starting transfers between devices, body(): lax.all_to_all(grad_share.reshape(expert_count, capacity, half_width), 'e...  14.6 us
    all_to_all x1, starting transfers between devices, body(): lax.all_to_all(score_full.reshape(expert_count, capacity), 'expert', spli...  13.7 us
    another operation x1, local copies, waits for them, and re-layouts, body(): rows_d = full[:, :, 1, :].reshape(slot_count, model_width)  9.82 us
  transfers between devices with their start and end apart: 4, of which 3 were waited for; matrix products, arithmetic and copies ran while one was open for 2% of the time, Pallas kernels for 0%

commit v1 on v0

--- a/solution.py
+++ b/solution.py
@@ -33,7 +33,9 @@
         expert_count, capacity, 2, half_width
     )
     recv = lax.all_to_all(send, "expert", split_axis=0, concat_axis=0, tiled=True)
-    full = lax.all_gather(recv, "hid", axis=3, tiled=True)
+    full = jnp.concatenate(
+        lax.all_to_all(jnp.stack([recv for _ in range(lax.axis_size("hid"))]), "hid", 0, 0), axis=3
+    )
     rows_x = full[:, :, 0, :].reshape(slot_count, model_width)
     rows_d = full[:, :, 1, :].reshape(slot_count, model_width)
     gate_mat = w_gate[0]

time: 490 us -> 464 us (0.947); the launches traced: 481 us -> 462 us
  waiting for transfers between devices: 112 us -> 89.5 us
  blocking collectives: 143 us -> 157 us
  local copies, waits for them, and re-layouts: 144 us -> 131 us
  other arithmetic: 9.33 us -> 19.8 us
  starting transfers between devices: 28.4 us -> 21.2 us
    slice x1 -> x2, local copies, waits for them, and re-layouts: 59.4 us -> 19.1 us  [body(): rows_d = full[:, :, 1, :].reshape(slot_count, model_width)]
    all_gather x1 -> x0, waiting for transfers between devices: 23.1 us -> none  [body(): full = lax.all_gather(recv, 'hid', axis=3, tiled=True)]
    all_to_all x0 -> x1, local copies, waits for them, and re-layouts: none -> 14.9 us  [body(): lax.all_to_all(jnp.stack([recv for _ in range(lax.axis_size('hid'))]), 'h...]
    all_to_all x0 -> x1, blocking collectives: none -> 14.1 us  [body(): lax.all_to_all(jnp.stack([recv for _ in range(lax.axis_size('hid'))]), 'h...]
    another operation x3 -> x4, other arithmetic: 0.26 us -> 10.7 us  [the longest x1 10.5 us: body(): jnp.stack([recv for _ in range(lax.axis_size('hid'))])]
    slice x0 -> x1, local copies, waits for them, and re-layouts: none -> 10.1 us  [body(): rows_x = full[:, :, 0, :].reshape(slot_count, model_width)]
    all_to_all x1, starting transfers between devices: 13.7 us -> 6.94 us  [body(): lax.all_to_all(score_full.reshape(expert_count, capacity), 'expert', spli...]
  transfers between devices with their start and end apart: 4 -> 3, of which waited for: 3 -> 2; matrix products, arithmetic and copies ran while one was open for 2% -> 2% of each run, Pallas kernels for 0% -> 0%
where the time goes in v1:
time: 464 us; the launch traced here: 462 us
  blocking collectives  157 us (34%)
  local copies, waits for them, and re-layouts  131 us (28%)
  waiting for transfers between devices  89.5 us (19%)
  matrix products  29.5 us (6%)
  starting transfers between devices  21.2 us (5%)
  other arithmetic  19.8 us (4%)
  between operations  14.3 us (3%)
    all_to_all x1, blocking collectives, body(): lax.all_to_all(send, 'expert', split_axis=0, concat_axis=0, tiled=True)  141 us
    all_to_all x1, waiting for transfers between devices, body(): lax.all_to_all(grad_share.reshape(expert_count, capacity, half_width), 'e...  81.2 us
    another operation x3, local copies, waits for them, and re-layouts, body(): jnp.stack([x_half[slot_token], d_half[slot_token]], axis=1)  33.3 us
    slice x2, local copies, waits for them, and re-layouts, body(): rows_d = full[:, :, 1, :].reshape(slot_count, model_width)  19.1 us
    all_to_all x1, local copies, waits for them, and re-layouts, body(): lax.all_to_all(jnp.stack([recv for _ in range(lax.axis_size('hid'))]), 'h...  14.9 us
    all_to_all x1, starting transfers between devices, body(): lax.all_to_all(grad_share.reshape(expert_count, capacity, half_width), 'e...  14.2 us
    all_to_all x1, blocking collectives, body(): lax.all_to_all(jnp.stack([recv for _ in range(lax.axis_size('hid'))]), 'h...  14.1 us
    another operation x1, other arithmetic, body(): jnp.stack([recv for _ in range(lax.axis_size('hid'))])  10.5 us
  transfers between devices with their start and end apart: 3, of which 2 were waited for; matrix products, arithmetic and copies ran while one was open for 2% of the time, Pallas kernels for 0%

profile of v1, /device:TPU:32, one launch (start us, length us, event | category | flops | bytes accessed | tf_op | source)
XLA Modules:
  0.0 462.1 jit_solution(13122906355646345245)
XLA Ops:
  13.5 4.1 gather_fusion
  17.6 5.4 %stack.16 = bf16[128,6,1,1792]{3,1,0,2:T(8,128)(2,1)} reshape(bf16[768,1792]{1,0:T(8,128)(2,1)} %gather_fusion) | data formatting | bytes 5505024 | tf_op jit(solution)/shard_map/stack | solution.py:32
  23.0 3.2 gather_fusion.1
  28.9 5.1 %pad_maximum_fusion.1 = bf16[128,6,2,1792]{3,1,0,2:T(8,128)(2,1)S(1)} fusion(bf16[128,6,1,1792]{3,1,0,2:T(8,128)(2,1)} %stack.17, bf16[128,6,1,1792]{3,1,0,2:T(8,128)(2,1)} %stack.16), kind=kLoop, calls=%fused_computation.6 | loop fusion | flops 2752512 | bytes 11010048 | tf_op jit(solution)/shard_map/stack | solution.py:32
  34.0 25.1 %copy.23 = bf16[128,6,2,1792]{3,2,1,0:T(2,128)(2,1)S(1)} copy(bf16[128,6,2,1792]{3,1,0,2:T(8,128)(2,1)S(1)} %pad_maximum_fusion.1) | data formatting | bytes 11010048 | tf_op jit(solution)/shard_map/stack | solution.py:32
  59.2 140.5 %all_to_all.25 = bf16[128,6,2,1792]{3,2,1,0:T(2,128)(2,1)S(1)} all-to-all(bf16[128,6,2,1792]{3,2,1,0:T(2,128)(2,1)S(1)} %copy.23), channel_id=1, replica_groups=mesh['expert'=128,'hid'=2] {'expert'}, dimensions={0} | all-to-all | bytes 11010048 | tf_op jit(solution)/shard_map/all_to_all | solution.py:35
  199.7 10.5 %pad_maximum_fusion = bf16[2,128,6,2,1792]{4,3,2,1,0:T(2,128)(2,1)S(1)} fusion(bf16[1,128,6,2,1792]{4,3,2,1,0:T(2,128)(2,1)S(1)} %bitcast.48), kind=kLoop, calls=%fused_computation.5 | loop fusion | flops 5505024 | bytes 16515072 | tf_op jit(solution)/shard_map/stack | solution.py:37
  212.8 14.1 %all_to_all.26 = bf16[2,128,6,2,1792]{4,1,3,2,0:T(8,128)(2,1)} all-to-all(bf16[2,128,6,2,1792]{4,1,3,2,0:T(8,128)(2,1)S(1)} %copy.24), channel_id=1, replica_groups=mesh['expert'=128,'hid'=2] {'hid'}, dimensions={0} | all-to-all | bytes 22020096 | tf_op jit(solution)/shard_map/all_to_all | solution.py:37
  226.8 14.9 %copy.25 = bf16[2,128,6,2,1792]{1,4,0,3,2:T(8,128)(2,1)} copy(bf16[2,128,6,2,1792]{4,1,3,2,0:T(8,128)(2,1)} %all_to_all.26) | data formatting | bytes 22020096 | tf_op jit(solution)/shard_map/all_to_all | solution.py:37
  241.7 8.9 %fusion.23 = (bf16[128,6,1,3584]{0,3,2,1:T(8,128)(2,1)}, bf16[128,6,1,3584]{0,3,2,1:T(8,128)(2,1)}) fusion(bf16[128,6,2,3584]{0,3,2,1:T(8,128)(2,1)} %bitcast.47), kind=kLoop, calls=%fused_computation.52 | loop fusion | bytes 22020096 | tf_op jit(solution)/shard_map/slice | solution.py:40
  250.6 10.1 %copy.27 = bf16[128,6,1,3584]{3,1,0,2:T(8,128)(2,1)} copy(bf16[128,6,1,3584]{0,3,2,1:T(8,128)(2,1)} %get-tuple-element.7) | data formatting | bytes 11010048 | tf_op jit(solution)/shard_map/slice | solution.py:39
  260.8 9.7 %reshape_squeeze.7 = bf16[768,3584]{1,0:T(8,128)(2,1)} reshape(bf16[128,6,1,3584]{3,1,0,2:T(8,128)(2,1)} %copy.27) | data formatting | bytes 11010048 | tf_op jit(solution)/shard_map/reshape;squeeze | solution.py:39
  270.4 6.9 %fusion.2 = f32[768,512]{0,1:T(8,128)S(1)} fusion(bf16[768,3584]{1,0:T(8,128)(2,1)} %reshape_squeeze.7, bf16[1,3584,512]{2,1,0:T(8,128)(2,1)} %param.11), kind=kOutput, calls=%fused_computation.10 | convolution fusion | flops 2818572288 | bytes 10747904 | tf_op jit(solution)/shard_map/dot_general | solution.py:45
  280.4 10.1 %copy.26 = bf16[128,6,1,3584]{3,1,0,2:T(8,128)(2,1)} copy(bf16[128,6,1,3584]{0,3,2,1:T(8,128)(2,1)} %get-tuple-element.6) | data formatting | bytes 11010048 | tf_op jit(solution)/shard_map/slice | solution.py:40
  290.5 9.7 %reshape_squeeze.6 = bf16[768,3584]{1,0:T(8,128)(2,1)} reshape(bf16[128,6,1,3584]{3,1,0,2:T(8,128)(2,1)} %copy.26) | data formatting | bytes 11010048 | tf_op jit(solution)/shard_map/reshape;squeeze | solution.py:40
  300.2 7.0 %multiply_reduce_fusion = (f32[768]{0:T(1024)S(1)}, f32[768,512]{0,1:T(8,128)S(1)}) fusion(f32[768,512]{0,1:T(8,128)S(1)} %fusion.5, f32[768,512]{0,1:T(8,128)S(1)} %fusion.2, bf16[768,3584]{1,0:T(8,128)(2,1)} %reshape_squeeze.6, bf16[1,512,3584]{2,1,0:T(8,128)(2,1)} %param.13), kind=kOutput, calls=%fused_computation.17 | convolution fusion | flops 2821324032 | bytes 13896704 | tf_op jit(solution)/shard_map/dot_general | solution.py:47
  307.2 3.6 fusion
  310.8 7.9 %convolution_add_fusion = f32[768,3584]{1,0:T(8,128)} fusion(f32[768,3584]{1,0:T(8,128)S(1)} %fusion, bf16[1,3584,512]{2,1,0:T(8,128)(2,1)} %param.12, f32[768,512]{0,1:T(8,128)S(1)} %get-tuple-element.9, f32[768,512]{0,1:T(8,128)S(1)} %fusion.2), kind=kOutput, calls=%fused_computation.7 | convolution fusion | flops 2823684096 | bytes 28835840 | tf_op jit(solution)/shard_map/dot_general | solution.py:59
  322.1 6.9 %all-to-all-start.3 = ((bf16[128,1,6]{2,1,0:T(2,128)(2,1)}), bf16[128,1,6]{2,1,0:T(2,128)(2,1)S(1)}, u32[]{:S(2)}, u32[]{:S(2)}) async-start(bf16[128,1,6]{2,1,0:T(2,128)(2,1)} %all_to_all.20), calls=%async_computation.4 | async-start | bytes 131072 | tf_op jit(solution)/shard_map/all_to_all | solution.py:72
  329.0 8.2 %reduce-scatter.2.cloned.1.call-done = f32[768,1792]{1,0:T(8,128)} async-done(((f32[768,3584]{1,0:T(8,128)}), f32[768,1792]{1,0:T(8,128)}) %reduce-scatter.2.cloned.1.call-update) | async-done | bytes 5505040 | tf_op jit(solution)/shard_map/reduce_scatter | solution.py:60
  342.7 14.2 %all-to-all-start.2 = ((bf16[128,6,1792]{2,1,0:T(8,128)(2,1)}), bf16[128,6,1792]{2,1,0:T(8,128)(2,1)}, u32[]{:S(2)}, u32[]{:S(2)}) async-start(bf16[128,6,1792]{2,1,0:T(8,128)(2,1)} %reshape.84), calls=%async_computation.3 | async-start | bytes 7340032 | tf_op jit(solution)/shard_map/all_to_all | solution.py:65
  357.5 3.5 gather_fusion.3
  361.8 81.2 %all-to-all-done.2 = bf16[128,6,1792]{2,1,0:T(8,128)(2,1)} async-done(((bf16[128,6,1792]{2,1,0:T(8,128)(2,1)}), bf16[128,6,1792]{2,1,0:T(8,128)(2,1)}, u32[]{:S(2)}, u32[]{:S(2)}) %all-to-all-start.2) | async-done | bytes 2752544 | tf_op jit(solution)/shard_map/all_to_all | solution.py:65
  443.0 4.0 reshape.85
  (49 shorter events, 32.9 us)
Async XLA Ops:
  7.2 330.0 %reduce-scatter.2.cloned.1.call-start = ((), (), s32[]{:S(2)}) async-start(), calls=%async_computation.5 | async-start | bytes 16515072 | tf_op jit(solution)/shard_map/reduce_scatter | solution.py:60
  270.4 6.9 %copy-start = (bf16[768,3584]{1,0:T(8,128)(2,1)S(1)}, bf16[768,3584]{1,0:T(8,128)(2,1)}, u32[]{:S(2)}) copy-start(bf16[768,3584]{1,0:T(8,128)(2,1)} %reshape_squeeze.7) | copy-start | bytes 16515076
  270.4 6.9 %copy-start.2 = (bf16[1,3584,512]{2,1,0:T(8,128)(2,1)S(1)}, bf16[1,3584,512]{2,1,0:T(8,128)(2,1)}, u32[]{:S(2)}) copy-start(bf16[1,3584,512]{2,1,0:T(8,128)(2,1)} %param.12) | copy-start | bytes 11010052
  300.2 7.0 %copy-start.1 = (bf16[1,3584,512]{2,1,0:T(8,128)(2,1)S(1)}, bf16[1,3584,512]{2,1,0:T(8,128)(2,1)}, u32[]{:S(2)}) copy-start(bf16[1,3584,512]{2,1,0:T(8,128)(2,1)} %param.11) | copy-start | bytes 11010052
  322.1 20.7 %all-to-all-start.3 = ((bf16[128,1,6]{2,1,0:T(2,128)(2,1)}), bf16[128,1,6]{2,1,0:T(2,128)(2,1)S(1)}, u32[]{:S(2)}, u32[]{:S(2)}) async-start(bf16[128,1,6]{2,1,0:T(2,128)(2,1)} %all_to_all.20), calls=%async_computation.4 | async-start | bytes 131072 | tf_op jit(solution)/shard_map/all_to_all | solution.py:72
  342.7 14.3 %copy-start.3 = (f32[128,4]{0,1:T(4,128)S(1)}, f32[128,4]{0,1:T(4,128)}, u32[]{:S(2)}) copy-start(f32[128,4]{0,1:T(4,128)} %param.10) | copy-start | bytes 6148
  342.7 100.3 %all-to-all-start.2 = ((bf16[128,6,1792]{2,1,0:T(8,128)(2,1)}), bf16[128,6,1792]{2,1,0:T(8,128)(2,1)}, u32[]{:S(2)}, u32[]{:S(2)}) async-start(bf16[128,6,1792]{2,1,0:T(8,128)(2,1)} %reshape.84), calls=%async_computation.3 | async-start | bytes 7340032 | tf_op jit(solution)/shard_map/all_to_all | solution.py:65
Sparse Core Ops, SparseCore 0:
  318.9 18.2 reduce-scatter.1
